TPU v7x, 512 devices: a whole 4x4x16 slice. The times are simulated.
512 devices in a mesh: dp: 32 (over y, z_hi, core), mp: 16 (over z_lo, x).
Axes of the slice: x: 4, y: 4, z: 16 (z_hi: 4, z_lo: 4; z = z_hi * 4 + z_lo), core: 2. Of those that a mesh axis runs over, the one named last changes fastest.
Arguments:
- inputs: bfloat16 [16384, 4096], P('mp', 'dp'), may hold values from -6 to 6
- cotangent: bfloat16 [16384, 4096], P('mp', 'dp'), may hold values from -6 to 6
- r_factor: bfloat16 [1, 128, 128, 128], P(None, 'mp'), may hold values from -0.5 to 0.5
- l_factor: bfloat16 [1, 128, 128, 128], P(None, 'mp'), may hold values from -0.5 to 0.5
Outputs:
- outputs: bfloat16 [16384, 4096], P('mp', 'dp')
- grad_inputs: bfloat16 [16384, 4096], P('mp', 'dp')
- grad_r: float32 [1, 128, 128, 128], P(None, 'mp', 'dp')
- grad_l: float32 [1, 128, 128, 128], P(None, 'mp', 'dp')
All inputs are finite; a program needn't handle non-finite values.
Results may differ from a plain program's by a relative error of at most 0.0063.
Values may be sent and summed in bfloat16 or wider, within the bound.
No kernel may reach another device: no remote copies, remote signals or barrier semaphores. Data moves between devices by JAX's collectives and lax.ppermute only.
A program may use at most 64 MiB of HBM per device.

v0:
```python
import jax
import jax.numpy as jnp
from jax import lax
from jax.sharding import PartitionSpec as P

LAYERS = 1


def activate(values):
    return jax.nn.gelu(values, approximate=True)


def second_product(received, left):
    return jnp.einsum("ijt,jim->jmt", received, left, preferred_element_type=jnp.float32)


def left_apply(left, received):
    return (received, second_product(received, left))


def first_product(current, right):
    return jnp.einsum("ikt,ikj->ijt", current, right, preferred_element_type=jnp.float32).astype(
        jnp.bfloat16
    )


def forward_layer(current, right, left):
    first_out = first_product(current, right)
    return left_apply(
        left, lax.all_to_all(first_out, "mp", split_axis=1, concat_axis=0, tiled=True)
    )


def shards(inputs, cotangent, r_factor, l_factor):
    block_count = r_factor.shape[1]
    block_size = r_factor.shape[2]
    tokens_here = inputs.shape[1]
    scale = float(lax.axis_size("dp") * tokens_here) ** (-0.5)
    current = inputs.reshape(block_count, block_size, tokens_here)
    layer_index = 0
    received, pre_act = forward_layer(current, r_factor[layer_index], l_factor[layer_index])
    saved = [(current, received, pre_act)]
    current = activate(pre_act).astype(jnp.bfloat16)
    outputs = current.reshape(block_count * block_size, tokens_here)
    grad_now = cotangent.reshape(block_count, block_size, tokens_here)
    parts_r = [None] * LAYERS
    parts_l = [None] * LAYERS
    for layer_index in reversed(range(LAYERS)):
        right = r_factor[layer_index]
        left = l_factor[layer_index]
        layer_in = saved[layer_index][0]
        received = saved[layer_index][1]
        pre_act = saved[layer_index][2]
        back_fn = jax.vjp(activate, pre_act)[1]
        grad_pre = back_fn(grad_now.astype(jnp.float32))[0].astype(jnp.bfloat16)
        term_l = (
            jnp.einsum("ijt,jmt->jim", received, grad_pre, preferred_element_type=jnp.float32)
            * scale
        )
        parts_l[layer_index] = lax.psum_scatter(term_l, "dp", scatter_dimension=1, tiled=True)
        grad_first = jnp.einsum(
            "jmt,jim->ijt", grad_pre, left, preferred_element_type=jnp.float32
        ).astype(jnp.bfloat16)

        def apply_back(returned, right=right):
            spread = jnp.einsum("ijt,ikj->ikt", returned, right, preferred_element_type=jnp.float32)
            return (returned, spread.astype(jnp.bfloat16))

        returned, grad_now = apply_back(
            lax.all_to_all(grad_first, "mp", split_axis=0, concat_axis=1, tiled=True)
        )
        term_r = (
            jnp.einsum("ikt,ijt->ikj", layer_in, returned, preferred_element_type=jnp.float32)
            * scale
        )
        parts_r[layer_index] = lax.psum_scatter(term_r, "dp", scatter_dimension=1, tiled=True)
    stack_r = jnp.stack(parts_r, 0)
    stack_l = jnp.stack(parts_l, 0)
    grad_inputs = grad_now.reshape(block_count * block_size, tokens_here)
    return (outputs, grad_inputs, stack_r, stack_l)


def solution(mesh):
    placed = (P("mp", "dp"), P("mp", "dp"), P(None, "mp", None, None), P(None, "mp", None, None))
    return jax.shard_map(
        shards,
        mesh=mesh,
        in_specs=placed,
        out_specs=(
            P("mp", "dp"),
            P("mp", "dp"),
            P(None, "mp", "dp", None),
            P(None, "mp", "dp", None),
        ),
        check_vma=False,
    )
```

profile of v0, /device:TPU:2, one launch (start us, length us, event | category | flops | bytes accessed | tf_op | source)
XLA Modules:
  0.0 270.8 jit_solution(16528090919166589030)
XLA Ops:
  7.2 0.0 copy-start
  7.2 1.3 convolution_convert_fusion.2
  8.5 0.2 copy.22
  8.7 0.0 copy-start.3
  8.7 18.1 %all_to_all.36 = bf16[8,128,128]{2,0,1:T(8,128)(2,1)S(1)} all-to-all(bf16[8,128,128]{2,0,1:T(8,128)(2,1)S(1)} %copy.22), channel_id=1, replica_groups=mesh['dp'=32,'mp'=16] {'mp'}, dimensions={1} | all-to-all | bytes 524288 | tf_op jit(solution)/shard_map/all_to_all | solution.py:30
  26.9 0.0 copy-done
  26.9 0.0 copy-done.3
  26.9 1.3 fusion.4
  28.2 0.3 fusion.1
  28.5 0.9 copy.26
  29.4 5.1 %all-to-all-start.1 = ((bf16[128,8,128]{2,1,0:T(8,128)(2,1)}), bf16[128,8,128]{2,1,0:T(8,128)(2,1)S(1)}, u32[]{:S(2)}, u32[]{:S(2)}) async-start(bf16[128,8,128]{2,1,0:T(8,128)(2,1)} %copy.26), calls=%async_computation.1 | async-start | bytes 524288 | tf_op jit(solution)/shard_map/all_to_all | solution.py:70
  34.6 0.0 reduce-scatter.5.cloned.1.call-start
  34.6 0.3 convolution_multiply_fusion
  34.9 1.1 copy.29
  36.0 0.0 copy-start.2
  36.0 0.0 reduce-scatter.5.cloned.1.call-update
  36.0 0.0 reduce-scatter.3.cloned.1.call-start
  36.1 7.1 %all-to-all-done.1 = bf16[128,8,128]{2,1,0:T(8,128)(2,1)S(1)} async-done(((bf16[128,8,128]{2,1,0:T(8,128)(2,1)}), bf16[128,8,128]{2,1,0:T(8,128)(2,1)S(1)}, u32[]{:S(2)}, u32[]{:S(2)}) %all-to-all-start.1) | async-done | bytes 262176 | tf_op jit(solution)/shard_map/all_to_all | solution.py:70
  43.2 0.0 copy-done.2
  43.2 0.3 fusion
  43.5 1.0 copy.28
  44.5 0.0 copy-start.1
  44.5 0.0 reduce-scatter.3.cloned.1.call-update
  44.5 108.3 %reduce-scatter.5.cloned.1.call-done = f32[8,4,128]{2,0,1:T(8,128)} async-done(((f32[8,128,128]{2,0,1:T(8,128)}), f32[8,4,128]{2,0,1:T(8,128)}) %reduce-scatter.5.cloned.1.call-update) | async-done | bytes 16400 | tf_op jit(solution)/shard_map/reduce_scatter | solution.py:60
  152.8 1.3 copy.31
  154.1 0.0 copy-done.1
  154.1 0.9 convolution_convert_fusion
  155.0 107.7 %reduce-scatter.3.cloned.1.call-done = f32[8,4,128]{2,0,1:T(8,128)} async-done(((f32[8,128,128]{2,0,1:T(8,128)}), f32[8,4,128]{2,0,1:T(8,128)}) %reduce-scatter.3.cloned.1.call-update) | async-done | bytes 16400 | tf_op jit(solution)/shard_map/reduce_scatter | solution.py:76
  262.7 1.3 copy.30
Async XLA Ops:
  7.2 19.7 %copy-start = (bf16[1,8,128,128]{3,2,1,0:T(8,128)(2,1)S(1)}, bf16[1,8,128,128]{3,2,1,0:T(8,128)(2,1)}, u32[]{:S(2)}) copy-start(bf16[1,8,128,128]{3,2,1,0:T(8,128)(2,1)} %param.7) | copy-start | bytes 786436
  8.7 18.2 %copy-start.3 = (bf16[1024,128]{1,0:T(8,128)(2,1)S(1)}, bf16[1024,128]{1,0:T(8,128)(2,1)}, u32[]{:S(2)}) copy-start(bf16[1024,128]{1,0:T(8,128)(2,1)} %param.5) | copy-start | bytes 786436
  29.4 13.8 %all-to-all-start.1 = ((bf16[128,8,128]{2,1,0:T(8,128)(2,1)}), bf16[128,8,128]{2,1,0:T(8,128)(2,1)S(1)}, u32[]{:S(2)}, u32[]{:S(2)}) async-start(bf16[128,8,128]{2,1,0:T(8,128)(2,1)} %copy.26), calls=%async_computation.1 | async-start | bytes 524288 | tf_op jit(solution)/shard_map/all_to_all | solution.py:70
  34.6 118.2 %reduce-scatter.5.cloned.1.call-start = ((), (), s32[]{:S(2)}) async-start(), calls=%async_computation.5 | async-start | bytes 540672 | tf_op jit(solution)/shard_map/reduce_scatter | solution.py:60
  36.0 7.2 %copy-start.2 = (bf16[1024,128]{1,0:T(8,128)(2,1)S(1)}, bf16[1024,128]{1,0:T(8,128)(2,1)}, u32[]{:S(2)}) copy-start(bf16[1024,128]{1,0:T(8,128)(2,1)} %param.4) | copy-start | bytes 786436
  36.0 226.7 %reduce-scatter.3.cloned.1.call-start = ((), (), s32[]{:S(2)}) async-start(), calls=%async_computation.4 | async-start | bytes 540672 | tf_op jit(solution)/shard_map/reduce_scatter | solution.py:76
  44.5 109.6 %copy-start.1 = (bf16[1,8,128,128]{3,2,1,0:T(8,128)(2,1)S(1)}, bf16[1,8,128,128]{3,2,1,0:T(8,128)(2,1)}, u32[]{:S(2)}) copy-start(bf16[1,8,128,128]{3,2,1,0:T(8,128)(2,1)} %param.6) | copy-start | bytes 786436
Sparse Core Ops, SparseCore 0:
  39.7 113.0 reduce-scatter.4
  157.1 105.5 reduce-scatter.2
where the time goes:
time: 271 us
  waiting for transfers between devices  223 us (82%)
  blocking collectives  18.1 us (7%)
  between operations  14.1 us (5%)
  local copies, waits for them, and re-layouts  5.83 us (2%)
  starting transfers between devices  5.21 us (2%)
  matrix products  4.5 us (2%)
    reduce_scatter x1, waiting for transfers between devices, shards(): lax.psum_scatter(term_l, 'dp', scatter_dimension=1, tiled=True)  108 us
    reduce_scatter x1, waiting for transfers between devices, shards(): lax.psum_scatter(term_r, 'dp', scatter_dimension=1, tiled=True)  108 us
    all_to_all x1, blocking collectives, forward_layer(): lax.all_to_all(first_out, 'mp', split_axis=1, concat_axis=0, tiled=True)  18.1 us
    all_to_all x1, waiting for transfers between devices, shards(): lax.all_to_all(grad_first, 'mp', split_axis=0, concat_axis=1, tiled=True)  7.1 us
  transfers between devices with their start and end apart: 3, of which 3 were waited for; matrix products, arithmetic and copies ran while one was open for 2% of the time, Pallas kernels for 0%

commit v1 on v0

--- a/solution.py
+++ b/solution.py
@@ -1,9 +1,19 @@
+import functools
 import jax
 import jax.numpy as jnp
 from jax import lax
 from jax.sharding import PartitionSpec as P
 
 LAYERS = 1
+
+
+def define_group(view, lane_axis, dim_i, pos_dim):
+    heard = jnp.stack(jnp.split(view, lax.axis_size(lane_axis), axis=dim_i), 0)
+    work_now = lax.all_to_all(heard, lane_axis, 0, 0)
+    return jnp.concatenate(work_now, pos_dim)
+
+
+row_play = functools.partial(define_group, lane_axis="mp", dim_i=1, pos_dim=0)
 
 
 def activate(values):
@@ -26,9 +36,7 @@
 
 def forward_layer(current, right, left):
     first_out = first_product(current, right)
-    return left_apply(
-        left, lax.all_to_all(first_out, "mp", split_axis=1, concat_axis=0, tiled=True)
-    )
+    return left_apply(left, row_play(first_out))
 
 
 def shards(inputs, cotangent, r_factor, l_factor):

time: 271 us -> 271 us (level)
  no operation moved by 1% of the time
where the time goes in v1:
time: 271 us
  waiting for transfers between devices  223 us (82%)
  blocking collectives  18.1 us (7%)
  between operations  14.2 us (5%)
  local copies, waits for them, and re-layouts  5.86 us (2%)
  starting transfers between devices  5.23 us (2%)
  matrix products  4.49 us (2%)
    reduce_scatter x1, waiting for transfers between devices, shards(): lax.psum_scatter(term_l, 'dp', scatter_dimension=1, tiled=True)  108 us
    reduce_scatter x1, waiting for transfers between devices, shards(): lax.psum_scatter(term_r, 'dp', scatter_dimension=1, tiled=True)  108 us
    all_to_all x1, blocking collectives, define_group(): work_now = lax.all_to_all(heard, lane_axis, 0, 0)  18.1 us
    all_to_all x1, waiting for transfers between devices, shards(): lax.all_to_all(grad_first, 'mp', split_axis=0, concat_axis=1, tiled=True)  7.1 us
  transfers between devices with their start and end apart: 3, of which 3 were waited for; matrix products, arithmetic and copies ran while one was open for 2% of the time, Pallas kernels for 0%

profile of v1, /device:TPU:2, one launch (start us, length us, event | category | flops | bytes accessed | tf_op | source)
XLA Modules:
  0.0 271.0 jit_solution(5714630141937464084)
XLA Ops:
  7.2 0.0 copy-start
  7.2 1.3 convolution_convert_fusion.2
  8.8 0.0 copy-start.3
  8.9 18.1 %all_to_all.23 = bf16[16,8,8,128]{3,2,1,0:T(8,128)(2,1)S(1)} all-to-all(bf16[16,8,8,128]{3,2,1,0:T(8,128)(2,1)S(1)} %constant_dynamic-update-slice_fusion), channel_id=1, replica_groups=mesh['dp'=32,'mp'=16] {'mp'}, dimensions={0} | all-to-all | bytes 524288 | tf_op jit(solution)/shard_map/all_to_all | solution.py:12
  27.0 0.0 copy-done
  27.0 0.0 copy-done.3
  27.0 1.3 fusion.4
  28.3 0.3 fusion.1
  28.6 0.9 copy.27
  29.5 5.1 %all-to-all-start.1 = ((bf16[128,8,128]{2,1,0:T(8,128)(2,1)}), bf16[128,8,128]{2,1,0:T(8,128)(2,1)S(1)}, u32[]{:S(2)}, u32[]{:S(2)}) async-start(bf16[128,8,128]{2,1,0:T(8,128)(2,1)} %copy.27), calls=%async_computation.1 | async-start | bytes 524288 | tf_op jit(solution)/shard_map/all_to_all | solution.py:78
  34.7 0.0 reduce-scatter.5.cloned.1.call-start
  34.7 0.3 convolution_multiply_fusion
  35.0 1.1 copy.31
  36.1 0.0 copy-start.2
  36.1 0.0 reduce-scatter.5.cloned.1.call-update
  36.2 0.0 reduce-scatter.3.cloned.1.call-start
  36.2 7.1 %all-to-all-done.1 = bf16[128,8,128]{2,1,0:T(8,128)(2,1)S(1)} async-done(((bf16[128,8,128]{2,1,0:T(8,128)(2,1)}), bf16[128,8,128]{2,1,0:T(8,128)(2,1)S(1)}, u32[]{:S(2)}, u32[]{:S(2)}) %all-to-all-start.1) | async-done | bytes 262176 | tf_op jit(solution)/shard_map/all_to_all | solution.py:78
  43.3 0.0 copy-done.2
  43.3 0.3 fusion
  43.6 1.0 copy.29
  44.6 0.0 copy-start.1
  44.6 0.0 reduce-scatter.3.cloned.1.call-update
  44.6 108.3 %reduce-scatter.5.cloned.1.call-done = f32[8,4,128]{2,0,1:T(8,128)} async-done(((f32[8,128,128]{2,0,1:T(8,128)}), f32[8,4,128]{2,0,1:T(8,128)}) %reduce-scatter.5.cloned.1.call-update) | async-done | bytes 16400 | tf_op jit(solution)/shard_map/reduce_scatter | solution.py:68
  152.9 1.3 copy.33
  154.3 0.0 copy-done.1
  154.3 0.9 convolution_convert_fusion
  155.2 107.6 %reduce-scatter.3.cloned.1.call-done = f32[8,4,128]{2,0,1:T(8,128)} async-done(((f32[8,128,128]{2,0,1:T(8,128)}), f32[8,4,128]{2,0,1:T(8,128)}) %reduce-scatter.3.cloned.1.call-update) | async-done | bytes 16400 | tf_op jit(solution)/shard_map/reduce_scatter | solution.py:84
  262.8 1.3 copy.32
  (16 shorter events, 0.2 us)
Async XLA Ops:
  7.2 19.8 %copy-start = (bf16[1,8,128,128]{3,2,1,0:T(8,128)(2,1)S(1)}, bf16[1,8,128,128]{3,2,1,0:T(8,128)(2,1)}, u32[]{:S(2)}) copy-start(bf16[1,8,128,128]{3,2,1,0:T(8,128)(2,1)} %param.7) | copy-start | bytes 786436
  8.8 18.2 %copy-start.3 = (bf16[1024,128]{1,0:T(8,128)(2,1)S(1)}, bf16[1024,128]{1,0:T(8,128)(2,1)}, u32[]{:S(2)}) copy-start(bf16[1024,128]{1,0:T(8,128)(2,1)} %param.5) | copy-start | bytes 786436
  29.5 13.8 %all-to-all-start.1 = ((bf16[128,8,128]{2,1,0:T(8,128)(2,1)}), bf16[128,8,128]{2,1,0:T(8,128)(2,1)S(1)}, u32[]{:S(2)}, u32[]{:S(2)}) async-start(bf16[128,8,128]{2,1,0:T(8,128)(2,1)} %copy.27), calls=%async_computation.1 | async-start | bytes 524288 | tf_op jit(solution)/shard_map/all_to_all | solution.py:78
  34.7 118.3 %reduce-scatter.5.cloned.1.call-start = ((), (), s32[]{:S(2)}) async-start(), calls=%async_computation.5 | async-start | bytes 540672 | tf_op jit(solution)/shard_map/reduce_scatter | solution.py:68
  36.1 7.2 %copy-start.2 = (bf16[1024,128]{1,0:T(8,128)(2,1)S(1)}, bf16[1024,128]{1,0:T(8,128)(2,1)}, u32[]{:S(2)}) copy-start(bf16[1024,128]{1,0:T(8,128)(2,1)} %param.4) | copy-start | bytes 786436
  36.2 226.6 %reduce-scatter.3.cloned.1.call-start = ((), (), s32[]{:S(2)}) async-start(), calls=%async_computation.4 | async-start | bytes 540672 | tf_op jit(solution)/shard_map/reduce_scatter | solution.py:84
  44.6 109.7 %copy-start.1 = (bf16[1,8,128,128]{3,2,1,0:T(8,128)(2,1)S(1)}, bf16[1,8,128,128]{3,2,1,0:T(8,128)(2,1)}, u32[]{:S(2)}) copy-start(bf16[1,8,128,128]{3,2,1,0:T(8,128)(2,1)} %param.6) | copy-start | bytes 786436
Sparse Core Ops, SparseCore 0:
  39.8 113.0 reduce-scatter.4
  157.3 105.4 reduce-scatter.2
